TPU v7x, 512 devices: a whole 4x8x8 slice. The times are simulated.
512 devices in a mesh: blk: 64 (over z_hi, y, core), seq: 4 (over x), mp: 2 (over z_lo).
Axes of the slice: x: 4, y: 8, z: 8 (z_hi: 4, z_lo: 2; z = z_hi * 2 + z_lo), core: 2. Of those that a mesh axis runs over, the one named last changes fastest.
Arguments:
- hidden: bfloat16 [8, 512, 1536], P(('mp', 'seq'), 'blk'), parts along dimension 0, may hold values from -6 to 6
- labels: int32 [4, 512], P('seq'), may hold values from 0 to 50303
- lengths: int32 [4, 8], P('seq'), may hold values from 1 to 256, 512 in all within a row
- owners: int32 [32], replicated, may hold values from 0 to 31, each once
- w_inner: bfloat16 [3072, 2, 3072], P('mp', None, 'blk'), parts along dimension 0, may hold values from -0.15625 to 0.15625
- w_bcdt: bfloat16 [3072, 304], P('mp'), parts along dimension 0, may hold values from -0.15625 to 0.15625
- conv_inner: float32 [8, 3072], P('mp', 'blk'), parts along dimension 0, may hold values from -3 to 3
- conv_bc: float32 [8, 256], P('mp'), parts along dimension 0, may hold values from -3 to 3
- dt_bias: float32 [96], P('mp'), parts along dimension 0, may hold values from -3 to 0.5
- decay_rate: float32 [96], P('mp'), parts along dimension 0, may hold values from 0.01 to 1
- d_skip: float32 [96], P('mp'), parts along dimension 0, may hold values from 0.5 to 2
- norm_gain: float32 [6144], P(('mp', 'blk')), parts along dimension 0, may hold values from 0.5 to 1.5
- w_out: bfloat16 [6144, 1536], P(('mp', 'blk')), parts along dimension 0, may hold values from -0.109375 to 0.109375
- final_gain: float32 [3072], P('mp'), parts along dimension 0, may hold values from 0.5 to 1.5
- w_head: bfloat16 [3072, 50304], P('mp', 'blk'), parts along dimension 0, may hold values from -0.33170174 to 0.33170174
Outputs:
- layer_out: bfloat16 [8, 512, 1536], P(('mp', 'seq'), 'blk'), parts along dimension 0
- token_logprob: float32 [8, 512], P(('mp', 'seq'), 'blk'), parts along dimension 0
- seq_logprob: float32 [64], P(('mp', 'seq')), parts along dimension 0
There are 2 independent parts, one for each index of `mp`. A program takes and returns all parts, laid end to end along the dimension named above; an argument that names none is the same for every part. Nothing has to cross between parts.
Inputs may be any that keep to these rules, and one draw needn't show every extreme that they name: The 8 lengths of a group sum to 512 and the longest is exactly 256. `owners`: every output slot is named once.
All inputs are finite; a program needn't handle non-finite values.
Results may differ from a plain program's by a relative error of at most 0.0055.
Values may be sent and summed in bfloat16 or wider, within the bound.
No kernel may reach another device: no remote copies, remote signals or barrier semaphores. Data moves between devices by JAX's collectives and lax.ppermute only.
A program may use at most 64 MiB of HBM per device.

v0:
```python
import jax
import jax.numpy as jnp
from jax import lax
from jax.sharding import PartitionSpec as P

D = 1536
HEADDIM = 64
NSTATE = 128
SCAN_BLOCK = 256
CONV = 4
EPSILON = 1e-05
HIGH = lax.Precision.HIGHEST


def segments_of(lengths, count):
    starts = jnp.cumsum(lengths, axis=-1) - lengths
    places = jnp.arange(count, dtype=jnp.int32)
    segment = jnp.sum((places[:, None] >= starts[None, :]).astype(jnp.int32), axis=-1) - 1
    first = jnp.take(starts, segment)
    return (segment, places - first)


def causal_conv(values, weights, position):
    total = values * weights[0]
    for shift_by in range(1, CONV):
        moved = jnp.concatenate(
            [jnp.zeros_like(values[:shift_by, :]), values[:-shift_by, :]], axis=0
        )
        total = (
            total + moved * weights[shift_by] * (position >= shift_by).astype(jnp.float32)[:, None]
        )
    return total


def final_norm(values, gain):
    widened = values.astype(jnp.float32)
    scale = lax.rsqrt(jnp.mean(widened * widened, axis=-1, keepdims=True) + EPSILON)
    return (widened * scale * gain).astype(jnp.bfloat16)


def shards(
    hidden,
    labels,
    lengths,
    owners,
    w_inner,
    w_bcdt,
    conv_inner,
    conv_bc,
    dt_bias,
    decay_rate,
    d_skip,
    norm_gain,
    w_out,
    final_gain,
    w_head,
):
    rows_own = hidden[0]
    rows_count = rows_own.shape[0]
    blk_count = lax.axis_size("blk")
    blk_index = lax.axis_index("blk")
    gathered = lax.all_gather(rows_own, "blk", axis=0, tiled=True)
    tokens_all = gathered.shape[0]
    channels = w_inner.shape[2]
    inner_total = channels * blk_count
    inner_proj = jnp.dot(
        gathered, w_inner.reshape(D, 2 * channels), preferred_element_type=jnp.float32
    ).astype(jnp.bfloat16)
    state_proj = jnp.dot(gathered, w_bcdt, preferred_element_type=jnp.float32).astype(jnp.bfloat16)
    gate_half = inner_proj[:, :channels].astype(jnp.float32)
    segment, position = segments_of(lengths[0], tokens_all)
    conv_value = jax.nn.silu(
        causal_conv(inner_proj[:, channels:].astype(jnp.float32), conv_inner, position)
    )
    conv_state = jax.nn.silu(
        causal_conv(state_proj[:, : 2 * NSTATE].astype(jnp.float32), conv_bc, position)
    )
    input_map = conv_state[:, :NSTATE]
    output_map = conv_state[:, NSTATE:]
    step_size = jax.nn.softplus(state_proj[:, 2 * NSTATE :].astype(jnp.float32) + dt_bias)
    log_heads = -(step_size * decay_rate)
    first_channel = blk_index * channels
    channel_head = (first_channel + jnp.arange(channels, dtype=jnp.int32)) // HEADDIM
    head_low = first_channel // HEADDIM
    head_high = (first_channel + channels - 1) // HEADDIM
    mask_high = (channel_head == head_high).astype(jnp.float32)
    mask_low = 1.0 - mask_high
    step_pair = jnp.concatenate(
        [
            lax.dynamic_slice_in_dim(step_size, head_low, 1, 1),
            lax.dynamic_slice_in_dim(step_size, head_high, 1, 1),
        ],
        axis=1,
    )
    log_pair = jnp.concatenate(
        [
            lax.dynamic_slice_in_dim(log_heads, head_low, 1, 1),
            lax.dynamic_slice_in_dim(log_heads, head_high, 1, 1),
        ],
        axis=1,
    )
    step_channel = step_pair[:, 0:1] * mask_low + step_pair[:, 1:2] * mask_high
    driven = conv_value * step_channel
    slot_masks = (mask_low, mask_high)
    blocks = tokens_all // SCAN_BLOCK
    order = jnp.arange(SCAN_BLOCK, dtype=jnp.int32)
    causal = order[:, None] >= order[None, :]

    def block_step(carry, inputs):
        carried, previous = carry
        drive_block, in_block, out_block, log_block, seg_block = inputs
        cumulative = jnp.cumsum(log_block, axis=0)
        gram = jnp.dot(out_block, in_block.T, precision=HIGH)
        same = (seg_block[:, None] == seg_block[None, :]) & causal
        result = jnp.zeros((SCAN_BLOCK, channels), jnp.float32)
        for slot_index in range(2):
            column = cumulative[:, slot_index]
            spread = jnp.minimum(column[:, None] - column[None, :], 0.0)
            weights = jnp.where(same, jnp.exp(spread), 0.0)
            result = result + jnp.dot(
                gram * weights, drive_block * slot_masks[slot_index], precision=HIGH
            )
        carried_in = carried * (seg_block[0] == previous).astype(jnp.float32)
        rising = jnp.exp(cumulative[:, 0:1]) * mask_low + jnp.exp(cumulative[:, 1:2]) * mask_high
        leading = (seg_block == seg_block[0]).astype(jnp.float32)[:, None]
        result = result + leading * rising * jnp.dot(out_block, carried_in.T, precision=HIGH)
        trailing = (seg_block == seg_block[-1]).astype(jnp.float32)[:, None]
        tail_low = jnp.exp(cumulative[-1:, 0:1] - cumulative[:, 0:1])
        tail_high = jnp.exp(cumulative[-1:, 1:2] - cumulative[:, 1:2])
        tail = tail_low * mask_low + tail_high * mask_high
        whole_block = (seg_block[-1] == seg_block[0]).astype(jnp.float32)
        carried_new = whole_block * rising[-1][:, None] * carried_in + jnp.dot(
            (drive_block * tail * trailing).T, in_block, precision=HIGH
        )
        return ((carried_new, seg_block[-1]), result)

    initial = (jnp.zeros((channels, NSTATE), jnp.float32), jnp.int32(-1))
    scan_inputs = (
        driven.reshape(blocks, SCAN_BLOCK, channels),
        input_map.reshape(blocks, SCAN_BLOCK, NSTATE),
        output_map.reshape(blocks, SCAN_BLOCK, NSTATE),
        log_pair.reshape(blocks, SCAN_BLOCK, 2),
        segment.reshape(blocks, SCAN_BLOCK),
    )
    final_carry, scanned = lax.scan(block_step, initial, scan_inputs)
    mixed = scanned.reshape(tokens_all, channels) + jnp.take(d_skip, channel_head) * conv_value
    gated = mixed * jax.nn.silu(gate_half)
    squares = lax.psum(jnp.sum(gated * gated, axis=1), "blk")
    inverse = lax.rsqrt(squares / inner_total + EPSILON)
    gated_norm = (gated * inverse[:, None] * norm_gain).astype(jnp.bfloat16)
    delta_own = lax.psum_scatter(
        jnp.dot(gated_norm, w_out, preferred_element_type=jnp.float32),
        "blk",
        scatter_dimension=0,
        tiled=True,
    )
    layer_own = (rows_own.astype(jnp.float32) + delta_own).astype(jnp.bfloat16)
    logits = jnp.dot(
        lax.all_gather(final_norm(layer_own, final_gain), "blk", axis=0, tiled=True),
        w_head,
        preferred_element_type=jnp.float32,
    )
    vocab_local = w_head.shape[1]
    local_label = labels[0] - blk_index * vocab_local
    hit = jnp.arange(vocab_local, dtype=jnp.int32)[None, :] == local_label[:, None]
    target_local = jnp.sum(jnp.where(hit, logits, 0.0), axis=1)
    top_local = jnp.max(logits, axis=1)
    top_all = lax.pmax(top_local, "blk")
    expsum_local = jnp.sum(jnp.exp(logits - top_all[:, None]), axis=1)
    expsum_all, target_all = lax.psum((expsum_local, target_local), "blk")
    logprob = target_all - (top_all + jnp.log(expsum_all))
    token_own = lax.dynamic_slice_in_dim(logprob, blk_index * rows_count, rows_count, 0)
    seqs_count = lengths.shape[1]
    onehot = (segment[:, None] == jnp.arange(seqs_count, dtype=jnp.int32)[None, :]).astype(
        jnp.float32
    )
    sums = jnp.dot(logprob, onehot, precision=HIGH)
    seq_index = lax.axis_index("seq")
    mine = lax.dynamic_slice_in_dim(owners, seq_index * seqs_count, seqs_count, 0)
    placement = (mine[:, None] == jnp.arange(owners.shape[0], dtype=jnp.int32)[None, :]).astype(
        jnp.float32
    )
    spread_sums = jnp.dot(sums, placement, precision=HIGH)
    seq_own = lax.psum_scatter(spread_sums, "seq", scatter_dimension=0, tiled=True)
    return (layer_own[None], token_own[None], seq_own)


def solution(mesh):
    in_specs = (
        P(("mp", "seq"), "blk", None),
        P("seq", None),
        P("seq", None),
        P(),
        P("mp", None, "blk"),
        P("mp", None),
        P("mp", "blk"),
        P("mp", None),
        P("mp"),
        P("mp"),
        P("mp"),
        P(("mp", "blk")),
        P(("mp", "blk"), None),
        P("mp"),
        P("mp", "blk"),
    )
    out_specs = (P(("mp", "seq"), "blk", None), P(("mp", "seq"), "blk"), P(("mp", "seq")))
    return jax.shard_map(shards, mesh=mesh, in_specs=in_specs, out_specs=out_specs, check_vma=False)
```

profile of v0, /device:TPU:1, one launch (start us, length us, event | category | flops | bytes accessed | tf_op | source)
XLA Modules:
  0.0 819.6 jit_solution(5413940078656478816)
XLA Ops:
  10.2 1.4 gather_fusion
  13.6 1.4 slice_bitcast_fusion.3
  15.0 4.4 compare_select_fusion.5
  21.0 80.3 %all-gather.6.cloned.1.call-done = bf16[1,512,1536]{2,1,0:T(8,128)(2,1)} async-done(((bf16[1,8,1536]{2,1,0:T(8,128)(2,1)}), bf16[1,512,1536]{2,1,0:T(8,128)(2,1)}) %all-gather.6.cloned.1.call-update) | async-done | bytes 1572880 | tf_op jit(solution)/shard_map/all_gather | solution.py:62
  101.3 2.3 fusion.71
  104.8 2.0 fusion.74
  108.1 29.1 %while.17 = (s32[]{:T(128)}, f32[48,128]{1,0:T(8,128)S(1)}, s32[]{:T(128)}, f32[2,256,48]{1,0,2:T(2,128)}, s32[2,256]{1,0:T(2,128)}, /*index=5*/f32[2,256,2]{1,2...) while((s32[]{:T(128)}, f32[48,128]{1,0:T(8,128)S(1)}, ...), condition=%wide.region_5.6_spmd.clone.clone.clone, body=%wide.region_2.5_spmd.clone.clone.clone.sunk | while | flops 215140816 | bytes 2177448 | solution.py:145
  113.8 1.3 constant_dynamic-slice_fusion.12
  115.1 1.9 compare_convert_fusion.10
  118.0 2.2 dynamic_update_slice.8
  125.0 1.3 fusion.130
  128.4 1.3 constant_dynamic-slice_fusion.12
  129.6 1.9 compare_convert_fusion.10
  132.5 2.2 dynamic_update_slice.8
  138.8 138.1 %psum.21 = f32[512]{0:T(512)S(1)} all-reduce(f32[512]{0:T(512)S(1)} %get-tuple-element.251), channel_id=1, replica_groups=mesh['blk'=64,'seq'=4,'mp'=2] {'blk'}, use_global_device_ids=true, to_apply=%region_7.8 | all-reduce | flops 512 | bytes 4096 | tf_op jit(solution)/shard_map/psum | solution.py:148
  276.9 3.0 fusion.85
  279.9 148.0 %reduce-scatter.2.cloned.1.call-done = f32[8,1536]{1,0:T(8,128)} async-done(((f32[512,1536]{1,0:T(8,128)}), f32[8,1536]{1,0:T(8,128)}) %reduce-scatter.2.cloned.1.call-update) | async-done | bytes 49168 | tf_op jit(solution)/shard_map/reduce_scatter | solution.py:151
  429.7 1.3 dynamic-slice
  431.7 85.4 %all-gather.4.cloned.1.call-done = bf16[512,1536]{1,0:T(8,128)(2,1)} async-done(((bf16[8,1536]{1,0:T(8,128)(2,1)}), bf16[512,1536]{1,0:T(8,128)(2,1)}) %all-gather.4.cloned.1.call-update) | async-done | bytes 1572880 | tf_op jit(solution)/shard_map/all_gather | solution.py:159
  517.1 4.0 fusion.101
  521.1 138.1 %pmax.7 = f32[512]{0:T(512)S(1)} all-reduce(f32[512]{0:T(512)S(1)} %get-tuple-element.299), channel_id=1, replica_groups=mesh['blk'=64,'seq'=4,'mp'=2] {'blk'}, use_global_device_ids=true, to_apply=%region_13.14 | all-reduce | flops 512 | bytes 4096 | tf_op jit(solution)/shard_map/pmax | solution.py:168
  659.2 1.9 exponential_reduce_fusion
  661.1 142.0 %all-reduce.7 = (f32[512]{0:T(512)S(1)}, f32[512]{0:T(512)S(1)}) all-reduce(f32[512]{0:T(512)S(1)} %get-tuple-element.222, f32[512]{0:T(512)S(1)} %get-tuple-element.221), channel_id=1, replica_groups=mesh['blk'=64,'seq'=4,'mp'=2] {'blk'}, use_global_device_ids=true, to_apply=%region_11.12 | all-reduce | flops 1024 | bytes 8192 | tf_op jit(solution)/shard_map/psum | solution.py:170
  803.6 8.4 %all-reduce.6 = f32[32]{0:T(128)S(1)} all-reduce(f32[32]{0:T(128)S(1)} %convolution_bitcast_fusion.1), channel_id=4, replica_groups=mesh['blk'=64,'seq'=4,'mp'=2] {'seq'}, use_global_device_ids=true, to_apply=%region_16.17.clone | all-reduce | flops 32 | bytes 256
  (135 shorter events, 25.4 us)
Async XLA Ops:
  7.2 509.9 %copy-start = (bf16[1536,786]{0,1:T(8,128)(2,1)S(1)}, bf16[1536,786]{0,1:T(8,128)(2,1)}, u32[]{:S(2)}) copy-start(bf16[1536,786]{0,1:T(8,128)(2,1)} %param.31) | copy-start | bytes 7243780
  7.2 94.1 %all-gather.6.cloned.1.call-start = ((), (), s32[]{:S(2)}) async-start(), calls=%async_computation.3 | async-start | bytes 1597440 | tf_op jit(solution)/shard_map/all_gather | solution.py:62
  7.9 420.1 %reduce-scatter.2.cloned.1.call-start = ((), (), s32[]{:S(2)}) async-start(), calls=%async_computation.1 | async-start | bytes 3194880 | tf_op jit(solution)/shard_map/reduce_scatter | solution.py:151
  9.6 94.1 %copy-start.5 = (s32[512]{0:T(512)}, s32[512]{0:T(512)S(1)}, u32[]{:S(2)}) copy-start(s32[512]{0:T(512)S(1)} %get-tuple-element.290) | copy-start | bytes 6148
  20.1 83.6 %copy-start.11 = (f32[512]{0:T(512)}, f32[512]{0:T(512)S(1)}, u32[]{:S(2)}) copy-start(f32[512]{0:T(512)S(1)} %get-tuple-element.257) | copy-start | bytes 6148
  20.1 83.6 %copy-start.7 = (f32[512]{0:T(512)}, f32[512]{0:T(512)S(1)}, u32[]{:S(2)}) copy-start(f32[512]{0:T(512)S(1)} %get-tuple-element.287) | copy-start | bytes 6148
  20.1 83.6 %copy-start.9 = (f32[512]{0:T(512)}, f32[512]{0:T(512)S(1)}, u32[]{:S(2)}) copy-start(f32[512]{0:T(512)S(1)} %get-tuple-element.288) | copy-start | bytes 6148
  104.7 2.3 copy-start.8
  104.7 2.3 copy-start.10
  104.8 2.3 copy-start.12
  104.8 2.3 copy-start.15
  104.8 2.3 copy-start.16
  104.8 2.3 copy-start.17
  104.8 2.3 copy-start.18
  104.8 2.3 copy-start.19
  104.8 2.3 copy-start.20
  108.1 168.8 %copy-start.1 = (bf16[48,1536]{1,0:T(8,128)(2,1)S(1)}, bf16[48,1536]{1,0:T(8,128)(2,1)}, u32[]{:S(2)}) copy-start(bf16[48,1536]{1,0:T(8,128)(2,1)} %param.29) | copy-start | bytes 442372
  279.9 148.1 %copy-start.4 = (bf16[1,8,1536]{2,1,0:T(8,128)(2,1)S(1)}, bf16[1,8,1536]{2,1,0:T(8,128)(2,1)}, u32[]{:S(2)}) copy-start(bf16[1,8,1536]{2,1,0:T(8,128)(2,1)} %param.17) | copy-start | bytes 73732
  279.9 149.1 %copy-start.13 = (f32[1536]{0:T(1024)S(1)}, f32[1536]{0:T(1024)}, u32[]{:S(2)}) copy-start(f32[1536]{0:T(1024)} %param.30) | copy-start | bytes 18436
  279.9 149.8 %copy-start.23 = (s32[32]{0:T(128)S(1)}, s32[32]{0:T(128)}, u32[]{:S(2)}) copy-start(s32[32]{0:T(128)} %param.20) | copy-start | bytes 388
  279.9 151.8 %copy-start.14 = (s32[1,512]{1,0:T(1,128)S(1)}, s32[1,512]{1,0:T(1,128)}, u32[]{:S(2)}) copy-start(s32[1,512]{1,0:T(1,128)} %param.18) | copy-start | bytes 6148
  279.9 237.2 %all-gather.4.cloned.1.call-start = ((), (), s32[]{:S(2)}) async-start(), calls=%async_computation.2 | async-start | bytes 1597440 | tf_op jit(solution)/shard_map/all_gather | solution.py:159
  428.9 92.2 %copy-start.3 = (bf16[8,1536]{1,0:T(8,128)(2,1)}, bf16[8,1536]{1,0:T(8,128)(2,1)S(1)}, u32[]{:S(2)}) copy-start(bf16[8,1536]{1,0:T(8,128)(2,1)S(1)} %get-tuple-element.250) | copy-start | bytes 73732
  521.1 282.0 %copy-start.6 = (s32[512]{0:T(512)S(1)}, s32[512]{0:T(512)}, u32[]{:S(2)}) copy-start(s32[512]{0:T(512)} %copy-done.5) | copy-start | bytes 6148
  (4 other events, 6.4 us)
Sparse Core Ops, SparseCore 0:
  11.3 89.9 all-gather.5
  280.0 147.9 reduce-scatter.1
  431.3 85.7 all-gather.3
where the time goes:
time: 821 us; the launch traced here: 820 us
  blocking collectives  427 us (52%)
  waiting for transfers between devices  314 us (38%)
  other arithmetic  22.4 us (3%)
  local copies, waits for them, and re-layouts  20.4 us (2%)
  matrix products  15.5 us (2%)
  between operations  14.9 us (2%)
    reduce_scatter x1, waiting for transfers between devices, shards(): lax.psum_scatter(jnp.dot(gated_norm, w_out, preferred_element_type=jnp.fl...  148 us
    psum x1, blocking collectives, shards(): expsum_all, target_all = lax.psum((expsum_local, target_local), 'blk')  142 us
    psum x1, blocking collectives, shards(): squares = lax.psum(jnp.sum(gated * gated, axis=1), 'blk')  138 us
    pmax x1, blocking collectives, shards(): top_all = lax.pmax(top_local, 'blk')  138 us
    all_gather x1, waiting for transfers between devices, shards(): lax.all_gather(final_norm(layer_own, final_gain), 'blk', axis=0, tiled=True)  85.4 us
    all_gather x1, waiting for transfers between devices, shards(): gathered = lax.all_gather(rows_own, 'blk', axis=0, tiled=True)  80.3 us
  transfers between devices with their start and end apart: 3, of which 3 were waited for; matrix products, arithmetic and copies ran while one was open for 2% of the time, Pallas kernels for 0%

commit v1 on v0

--- a/solution.py
+++ b/solution.py
@@ -155,8 +155,11 @@
         tiled=True,
     )
     layer_own = (rows_own.astype(jnp.float32) + delta_own).astype(jnp.bfloat16)
+    update_stops_all = lambda page, out_dim: jnp.concatenate(
+        lax.all_to_all(jnp.stack([page] * lax.axis_size("blk")), "blk", 0, 0), out_dim
+    )
     logits = jnp.dot(
-        lax.all_gather(final_norm(layer_own, final_gain), "blk", axis=0, tiled=True),
+        update_stops_all(final_norm(layer_own, final_gain), 0),
         w_head,
         preferred_element_type=jnp.float32,
     )

time: 821 us -> 787 us (0.959)
  waiting for transfers between devices: 314 us -> 267 us
  starting transfers between devices: 0.12 us -> 13.8 us
    all_gather x1 -> x0, waiting for transfers between devices: 85.4 us -> none  [shards(): lax.all_gather(final_norm(layer_own, final_gain), 'blk', axis=0, tiled=True)]
    all_to_all x0 -> x1, waiting for transfers between devices: none -> 38.4 us  [shards(): lax.all_to_all(jnp.stack([page] * lax.axis_size('blk')), 'blk', 0, 0)]
    all_to_all x0 -> x1, starting transfers between devices: none -> 13.7 us  [shards(): lax.all_to_all(jnp.stack([page] * lax.axis_size('blk')), 'blk', 0, 0)]
where the time goes in v1:
time: 787 us; the launch traced here: 786 us
  blocking collectives  425 us (54%)
  waiting for transfers between devices  267 us (34%)
  local copies, waits for them, and re-layouts  21.7 us (3%)
  other arithmetic  21.7 us (3%)
  matrix products  15.5 us (2%)
  between operations  15.2 us (2%)
  starting transfers between devices  13.8 us (2%)
    reduce_scatter x1, waiting for transfers between devices, shards(): lax.psum_scatter(jnp.dot(gated_norm, w_out, preferred_element_type=jnp.fl...  148 us
    pmax x1, blocking collectives, shards(): top_all = lax.pmax(top_local, 'blk')  140 us
    psum x1, blocking collectives, shards(): expsum_all, target_all = lax.psum((expsum_local, target_local), 'blk')  139 us
    psum x1, blocking collectives, shards(): squares = lax.psum(jnp.sum(gated * gated, axis=1), 'blk')  138 us
    all_gather x1, waiting for transfers between devices, shards(): gathered = lax.all_gather(rows_own, 'blk', axis=0, tiled=True)  80.4 us
    all_to_all x1, waiting for transfers between devices, shards(): lax.all_to_all(jnp.stack([page] * lax.axis_size('blk')), 'blk', 0, 0)  38.4 us
  transfers between devices with their start and end apart: 3, of which 3 were waited for; matrix products, arithmetic and copies ran while one was open for 2% of the time, Pallas kernels for 0%

profile of v1, /device:TPU:1, one launch (start us, length us, event | category | flops | bytes accessed | tf_op | source)
XLA Modules:
  0.0 785.6 jit_solution(2286627886554938423)
XLA Ops:
  10.2 1.4 gather_fusion
  13.6 1.4 slice_bitcast_fusion.3
  15.0 4.3 compare_select_fusion.5
  20.9 80.4 %all-gather.3.cloned.1.call-done = bf16[1,512,1536]{2,1,0:T(8,128)(2,1)} async-done(((bf16[1,8,1536]{2,1,0:T(8,128)(2,1)}), bf16[1,512,1536]{2,1,0:T(8,128)(2,1)}) %all-gather.3.cloned.1.call-update) | async-done | bytes 1572880 | tf_op jit(solution)/shard_map/all_gather | solution.py:62
  101.3 2.3 fusion.73
  104.8 2.0 fusion.76
  108.1 29.2 %while.17 = (s32[]{:T(128)}, f32[48,128]{1,0:T(8,128)S(1)}, s32[]{:T(128)}, f32[2,256,48]{1,0,2:T(2,128)}, s32[2,256]{1,0:T(2,128)}, /*index=5*/f32[2,256,2]{1,2...) while((s32[]{:T(128)}, f32[48,128]{1,0:T(8,128)S(1)}, ...), condition=%wide.region_5.6_spmd.clone.clone.clone, body=%wide.region_2.5_spmd.clone.clone.clone.sunk | while | flops 215140816 | bytes 2177448 | solution.py:145
  113.8 1.3 constant_dynamic-slice_fusion.12
  115.1 2.0 compare_convert_fusion.10
  118.0 2.2 dynamic_update_slice.8
  128.3 1.3 constant_dynamic-slice_fusion.12
  129.6 2.0 compare_convert_fusion.10
  132.6 2.2 dynamic_update_slice.8
  138.8 138.1 %psum.21 = f32[512]{0:T(512)S(1)} all-reduce(f32[512]{0:T(512)S(1)} %get-tuple-element.251), channel_id=1, replica_groups=mesh['blk'=64,'seq'=4,'mp'=2] {'blk'}, use_global_device_ids=true, to_apply=%region_7.8 | all-reduce | flops 512 | bytes 4096 | tf_op jit(solution)/shard_map/psum | solution.py:148
  276.9 3.0 fusion.87
  279.9 147.8 %reduce-scatter.2.cloned.1.call-done = f32[8,1536]{1,0:T(8,128)} async-done(((f32[512,1536]{1,0:T(8,128)}), f32[8,1536]{1,0:T(8,128)}) %reduce-scatter.2.cloned.1.call-update) | async-done | bytes 49168 | tf_op jit(solution)/shard_map/reduce_scatter | solution.py:151
  428.8 1.3 stack.2
  430.1 13.7 %all-to-all-start = ((bf16[64,8,1536]{2,1,0:T(8,128)(2,1)}), bf16[64,8,1536]{2,1,0:T(8,128)(2,1)}, u32[]{:S(2)}, u32[]{:S(2)}) async-start(bf16[64,8,1536]{2,1,0:T(8,128)(2,1)} %stack.2), calls=%async_computation.1 | async-start | bytes 3145728 | tf_op jit(solution)/shard_map/all_to_all | solution.py:159
  445.9 38.4 %all-to-all-done = bf16[64,8,1536]{2,1,0:T(8,128)(2,1)} async-done(((bf16[64,8,1536]{2,1,0:T(8,128)(2,1)}), bf16[64,8,1536]{2,1,0:T(8,128)(2,1)}, u32[]{:S(2)}, u32[]{:S(2)}) %all-to-all-start) | async-done | bytes 1572896 | tf_op jit(solution)/shard_map/all_to_all | solution.py:159
  484.3 4.0 fusion.103
  488.3 139.6 %pmax.7 = f32[512]{0:T(512)S(1)} all-reduce(f32[512]{0:T(512)S(1)} %get-tuple-element.299), channel_id=1, replica_groups=mesh['blk'=64,'seq'=4,'mp'=2] {'blk'}, use_global_device_ids=true, to_apply=%region_13.14 | all-reduce | flops 512 | bytes 4096 | tf_op jit(solution)/shard_map/pmax | solution.py:171
  627.8 1.9 exponential_reduce_fusion
  629.7 139.0 %all-reduce.7 = (f32[512]{0:T(512)S(1)}, f32[512]{0:T(512)S(1)}) all-reduce(f32[512]{0:T(512)S(1)} %get-tuple-element.222, f32[512]{0:T(512)S(1)} %get-tuple-element.221), channel_id=1, replica_groups=mesh['blk'=64,'seq'=4,'mp'=2] {'blk'}, use_global_device_ids=true, to_apply=%region_11.12 | all-reduce | flops 1024 | bytes 8192 | tf_op jit(solution)/shard_map/psum | solution.py:173
  769.2 8.4 %all-reduce.6 = f32[32]{0:T(128)S(1)} all-reduce(f32[32]{0:T(128)S(1)} %convolution_bitcast_fusion.1), channel_id=4, replica_groups=mesh['blk'=64,'seq'=4,'mp'=2] {'seq'}, use_global_device_ids=true, to_apply=%region_16.17.clone | all-reduce | flops 32 | bytes 256
  (135 shorter events, 27.1 us)
Async XLA Ops:
  7.2 477.1 %copy-start = (bf16[1536,786]{0,1:T(8,128)(2,1)S(1)}, bf16[1536,786]{0,1:T(8,128)(2,1)}, u32[]{:S(2)}) copy-start(bf16[1536,786]{0,1:T(8,128)(2,1)} %param.31) | copy-start | bytes 7243780
  7.2 94.1 %all-gather.3.cloned.1.call-start = ((), (), s32[]{:S(2)}) async-start(), calls=%async_computation.3 | async-start | bytes 1597440 | tf_op jit(solution)/shard_map/all_gather | solution.py:62
  7.9 419.9 %reduce-scatter.2.cloned.1.call-start = ((), (), s32[]{:S(2)}) async-start(), calls=%async_computation.2 | async-start | bytes 3194880 | tf_op jit(solution)/shard_map/reduce_scatter | solution.py:151
  9.6 94.1 %copy-start.5 = (s32[512]{0:T(512)}, s32[512]{0:T(512)S(1)}, u32[]{:S(2)}) copy-start(s32[512]{0:T(512)S(1)} %get-tuple-element.290) | copy-start | bytes 6148
  20.0 83.7 %copy-start.11 = (f32[512]{0:T(512)}, f32[512]{0:T(512)S(1)}, u32[]{:S(2)}) copy-start(f32[512]{0:T(512)S(1)} %get-tuple-element.257) | copy-start | bytes 6148
  20.0 83.7 %copy-start.7 = (f32[512]{0:T(512)}, f32[512]{0:T(512)S(1)}, u32[]{:S(2)}) copy-start(f32[512]{0:T(512)S(1)} %get-tuple-element.287) | copy-start | bytes 6148
  20.1 83.7 %copy-start.9 = (f32[512]{0:T(512)}, f32[512]{0:T(512)S(1)}, u32[]{:S(2)}) copy-start(f32[512]{0:T(512)S(1)} %get-tuple-element.288) | copy-start | bytes 6148
  104.7 2.2 copy-start.21
  104.8 2.3 copy-start.8
  104.8 2.3 copy-start.10
  104.8 2.3 copy-start.12
  104.8 2.3 copy-start.15
  104.8 2.3 copy-start.16
  104.8 2.3 copy-start.17
  104.8 2.3 copy-start.18
  104.8 2.3 copy-start.19
  104.8 2.3 copy-start.20
  108.1 168.9 %copy-start.1 = (bf16[48,1536]{1,0:T(8,128)(2,1)S(1)}, bf16[48,1536]{1,0:T(8,128)(2,1)}, u32[]{:S(2)}) copy-start(bf16[48,1536]{1,0:T(8,128)(2,1)} %param.29) | copy-start | bytes 442372
  279.9 147.8 %copy-start.4 = (bf16[1,8,1536]{2,1,0:T(8,128)(2,1)S(1)}, bf16[1,8,1536]{2,1,0:T(8,128)(2,1)}, u32[]{:S(2)}) copy-start(bf16[1,8,1536]{2,1,0:T(8,128)(2,1)} %param.17) | copy-start | bytes 73732
  279.9 148.8 %copy-start.13 = (f32[1536]{0:T(1024)S(1)}, f32[1536]{0:T(1024)}, u32[]{:S(2)}) copy-start(f32[1536]{0:T(1024)} %param.30) | copy-start | bytes 18436
  430.1 13.8 %copy-start.23 = (s32[32]{0:T(128)S(1)}, s32[32]{0:T(128)}, u32[]{:S(2)}) copy-start(s32[32]{0:T(128)} %param.20) | copy-start | bytes 388
  430.1 15.8 %copy-start.14 = (s32[1,512]{1,0:T(1,128)S(1)}, s32[1,512]{1,0:T(1,128)}, u32[]{:S(2)}) copy-start(s32[1,512]{1,0:T(1,128)} %param.18) | copy-start | bytes 6148
  430.1 54.2 %all-to-all-start = ((bf16[64,8,1536]{2,1,0:T(8,128)(2,1)}), bf16[64,8,1536]{2,1,0:T(8,128)(2,1)}, u32[]{:S(2)}, u32[]{:S(2)}) async-start(bf16[64,8,1536]{2,1,0:T(8,128)(2,1)} %stack.2), calls=%async_computation.1 | async-start | bytes 3145728 | tf_op jit(solution)/shard_map/all_to_all | solution.py:159
  488.3 280.4 %copy-start.6 = (s32[512]{0:T(512)S(1)}, s32[512]{0:T(512)}, u32[]{:S(2)}) copy-start(s32[512]{0:T(512)} %copy-done.5) | copy-start | bytes 6148
  (4 other events, 5.6 us)
Sparse Core Ops, SparseCore 0:
  11.3 89.9 all-gather.2
  280.1 147.6 reduce-scatter.1
